TPU v7x, 256 devices: a whole 4x4x8 slice. The times are simulated.
256 devices in a mesh: chan: 32 (over y_hi, z, core), win: 8 (over x, y_lo).
Axes of the slice: x: 4, y: 4 (y_hi: 2, y_lo: 2; y = y_hi * 2 + y_lo), z: 8, core: 2. Of those that a mesh axis runs over, the one named last changes fastest.
Arguments:
- traces: bfloat16 [8, 1024, 8192], P('win', 'chan'), may hold values from -6 to 6
- owner: int32 [3], replicated, may hold values from 0 to 31
- window_mask: int32 [8, 32], P('win', 'chan'), may hold values 0 or 1
Outputs:
- stacks: float32 [3, 32, 64, 1024], P(None, None, 'win', 'chan')
Inputs may be any that keep to these rules, and one draw needn't show every extreme that they name: `owner`: each step names one channel block.
All inputs are finite; a program needn't handle non-finite values. No bound on the sum of `window_mask` on one device may be relied on, other than what follows from the above.
Results may differ from a plain program's by a relative error of at most 0.0028.
Values may be sent and summed in bfloat16 or wider, within the bound.
No kernel may reach another device: no remote copies, remote signals or barrier semaphores. Data moves between devices by JAX's collectives and lax.ppermute only.
A program may use at most 128 MiB of HBM per device.

v0:
```python
import math
import jax
import jax.numpy as jnp
from jax import lax
from jax.sharding import PartitionSpec as P

LAGS = 64


def spread(value, axis, source):
    kept = jnp.where(lax.axis_index(axis) == source, value, 0).astype(value.dtype)
    return lax.psum(kept, axis)


def body(traces, owner, window_mask):
    chan_dev = traces.shape[1]
    samples = traces.shape[2]
    step_count = owner.shape[0]
    signal = traces[0].astype(jnp.float32)
    whitened = (
        signal * lax.rsqrt(jnp.mean(signal * signal, axis=-1, keepdims=True) + 1e-06)
    ).astype(jnp.bfloat16)
    own_flag = window_mask[0, 0].astype(jnp.float32)
    outgoing = whitened * own_flag.astype(jnp.bfloat16)
    received = [spread(outgoing, "chan", owner[step]) for step in range(step_count)]
    sources = jnp.concatenate(received, 0)
    padded = jnp.pad(whitened, ((0, 0), (64, 64)))
    half_lags = LAGS // 2
    win_count = lax.axis_size("win")
    per_dev = LAGS // win_count
    time_block = min(samples, 4096)
    factor = own_flag / math.sqrt(samples)

    def group_lags(which):
        return list(range(which * 8, which * 8 + 8))

    def correlate(lag_values):
        summed = jnp.zeros((sources.shape[0], len(lag_values), chan_dev), jnp.float32)
        for offset in range(0, samples, time_block):
            shifted = jnp.stack(
                [
                    padded[
                        :,
                        offset + lag - half_lags + 64 : offset + lag - half_lags + 64 + time_block,
                    ]
                    for lag in lag_values
                ],
                0,
            )
            summed = summed + jnp.einsum(
                "pt,gct->pgc",
                sources[:, offset : offset + time_block],
                shifted,
                preferred_element_type=jnp.float32,
            )
        return summed * factor

    complete = jnp.concatenate([correlate(group_lags(which)) for which in range(LAGS // 8)], 1)
    reduced = lax.psum_scatter(complete, "win", scatter_dimension=1, tiled=True)
    return reduced.reshape(step_count, chan_dev, per_dev, chan_dev)


def solution(mesh):
    return jax.shard_map(
        body,
        mesh=mesh,
        in_specs=(P("win", "chan", None), P(), P("win", "chan")),
        out_specs=P(None, None, "win", "chan"),
        check_vma=False,
    )
```

profile of v0, /device:TPU:16, one launch (start us, length us, event | category | flops | bytes accessed | tf_op | source)
XLA Modules:
  0.0 365.3 jit_solution(5036008442695685828)
XLA Ops:
  7.2 1.3 fusion.16
  8.5 1.4 fusion.27
  11.8 2.1 broadcast_select_fusion
  13.9 1.1 broadcast_select_fusion.1
  20.3 1.3 copy-done.20
  22.7 1.0 copy-done.14
  23.7 2.1 constant_dynamic-update-slice_fusion.123
  27.4 1.3 constant_dynamic-update-slice_fusion.107
  28.7 1.6 constant_dynamic-update-slice_fusion.91
  30.8 1.3 constant_dynamic-update-slice_fusion.75
  32.0 1.0 constant_dynamic-update-slice_fusion.54
  34.7 1.2 constant_dynamic-update-slice_fusion.51
  37.6 1.0 constant_dynamic-update-slice_fusion.35
  40.3 248.7 %all-reduce.4.cloned.1.call-done = (bf16[32,8192]{1,0:T(8,128)(2,1)}, bf16[32,8192]{1,0:T(8,128)(2,1)}, bf16[32,8192]{1,0:T(8,128)(2,1)}) async-done(((bf16[32,8192]{1,0:T(8,128)(2,1)}, bf16[32,8192]{1,0:T(8,128)(2,1)}, bf16[32,8192]{1,0:T(8,128)(2,1)}), (bf16[32,8192]{1,0:T(8,128)(2,1)}, bf16[32,8192]{1,0:T(8,128)(2,1)}, bf16[32,8192]{1,0:T(8,128)(2,1)})) %all-reduce.4.cloned.1.call-update) | async-done | bytes 1572880 | tf_op jit(solution)/shard_map/psum | solution.py:12
  289.1 1.2 constant_dynamic-update-slice_fusion.2
  290.3 1.1 constant_dynamic-update-slice_fusion.1
  291.4 1.2 constant_dynamic-update-slice_fusion
  293.3 0.9 fusion.19
  297.4 2.3 fusion.22
  299.7 2.3 fusion.23
  302.0 2.4 fusion.24
  313.9 1.0 copy-done.24
  314.9 41.8 %reduce-scatter.2.cloned.1.call-done = f32[96,8,32]{0,2,1:T(8,128)} async-done(((f32[96,64,32]{0,2,1:T(8,128)}), f32[96,8,32]{0,2,1:T(8,128)}) %reduce-scatter.2.cloned.1.call-update) | async-done | bytes 98320 | tf_op jit(solution)/shard_map/reduce_scatter | solution.py:59
  356.6 1.8 copy.6
  (95 shorter events, 26.5 us)
Async XLA Ops:
  6.5 282.5 %all-reduce.4.cloned.1.call-start = ((), (), s32[]{:S(2)}) async-start(), calls=%async_computation.2 | async-start | bytes 3145728 | tf_op jit(solution)/shard_map/psum | solution.py:12
  15.0 341.6 %reduce-scatter.2.cloned.1.call-start = ((), (), s32[]{:S(2)}) async-start(), calls=%async_computation.1 | async-start | bytes 1179648 | tf_op jit(solution)/shard_map/reduce_scatter | solution.py:59
  20.3 2.0 copy-start.22
  22.4 3.4 copy-start
  22.4 3.4 copy-start.2
  22.4 5.0 %copy-start.4 = (bf16[8,32,4096]{2,1,0:T(8,128)(2,1)}, bf16[8,32,4096]{2,1,0:T(8,128)(2,1)S(1)}, u32[]{:S(2)}) copy-start(bf16[8,32,4096]{2,1,0:T(8,128)(2,1)S(1)} %get-tuple-element.22) | copy-start | bytes 6291460
  22.4 5.0 %copy-start.6 = (bf16[8,32,4096]{2,1,0:T(8,128)(2,1)}, bf16[8,32,4096]{2,1,0:T(8,128)(2,1)S(1)}, u32[]{:S(2)}) copy-start(bf16[8,32,4096]{2,1,0:T(8,128)(2,1)S(1)} %get-tuple-element.24) | copy-start | bytes 6291460
  22.4 5.0 %copy-start.16 = (bf16[8,32,4096]{2,1,0:T(8,128)(2,1)}, bf16[8,32,4096]{2,1,0:T(8,128)(2,1)S(1)}, u32[]{:S(2)}) copy-start(bf16[8,32,4096]{2,1,0:T(8,128)(2,1)S(1)} %get-tuple-element.26) | copy-start | bytes 6291460
  25.7 4.6 %copy-start.10 = (bf16[8,32,4096]{2,1,0:T(8,128)(2,1)}, bf16[8,32,4096]{2,1,0:T(8,128)(2,1)S(1)}, u32[]{:S(2)}) copy-start(bf16[8,32,4096]{2,1,0:T(8,128)(2,1)S(1)} %get-tuple-element.10) | copy-start | bytes 6291460
  28.7 2.0 copy-start.18
  30.3 1.7 copy-start.12
  32.0 4.7 %copy-start.8 = (bf16[8,32,4096]{2,1,0:T(8,128)(2,1)}, bf16[8,32,4096]{2,1,0:T(8,128)(2,1)S(1)}, u32[]{:S(2)}) copy-start(bf16[8,32,4096]{2,1,0:T(8,128)(2,1)S(1)} %get-tuple-element.104) | copy-start | bytes 6291460
  289.1 3.6 copy-start.1
  291.4 2.0 copy-start.3
  293.3 1.6 copy-start.5
  294.2 1.7 copy-start.7
  302.0 2.5 copy-start.23
  304.4 1.6 copy-start.21
  305.2 1.7 copy-start.17
  306.7 1.6 copy-start.15
  307.6 1.7 copy-start.9
  309.1 1.7 copy-start.13
  310.1 1.7 copy-start.19
  311.5 1.7 copy-start.11
  (3 other events, 3.7 us)
Sparse Core Ops, SparseCore 0:
  15.1 273.8 all-reduce.3
  315.0 41.5 reduce-scatter.1
where the time goes:
time: 366 us; the launch traced here: 365 us
  waiting for transfers between devices  291 us (80%)
  local copies, waits for them, and re-layouts  37.4 us (10%)
  between operations  16.6 us (5%)
  matrix products  16.3 us (4%)
  other arithmetic  4.4 us (1%)
    psum x1, waiting for transfers between devices, spread(): return lax.psum(kept, axis)  249 us
    reduce_scatter x1, waiting for transfers between devices, body(): reduced = lax.psum_scatter(complete, 'win', scatter_dimension=1, tiled=True)  41.8 us
    unnamed x83, local copies, waits for them, and re-layouts  23.7 us
    dot_general x16, matrix products, correlate(): jnp.einsum('pt,gct->pgc', sources[:, offset:offset + time_block], shifted...  16.3 us
    another operation x7, local copies, waits for them, and re-layouts, correlate(): jnp.stack([padded[:, offset + lag - half_lags + 64:offset + lag - half_la...  9.25 us
  transfers between devices with their start and end apart: 2, of which 2 were waited for; matrix products, arithmetic and copies ran while one was open for 6% of the time, Pallas kernels for 0%

commit v1 on v0

--- a/solution.py
+++ b/solution.py
@@ -7,9 +7,14 @@
 LAGS = 64
 
 
+def derive_regions(t0, row_axis):
+    q_next = jnp.sum(lax.all_gather(t0, axis_name=row_axis), axis=0)
+    return q_next
+
+
 def spread(value, axis, source):
     kept = jnp.where(lax.axis_index(axis) == source, value, 0).astype(value.dtype)
-    return lax.psum(kept, axis)
+    return derive_regions(kept, axis)
 
 
 def body(traces, owner, window_mask):

time: 366 us -> 511 us (1.40)
  waiting for transfers between devices: 291 us -> 410 us
  other arithmetic: 4.4 us -> 32.1 us
    all_gather x0 -> x3, waiting for transfers between devices: none -> 367 us  [derive_regions(): q_next = jnp.sum(lax.all_gather(t0, axis_name=row_axis), axis=0)]
    psum x1 -> x0, waiting for transfers between devices: 249 us -> none  [spread(): return lax.psum(kept, axis)]
    reduce_sum x0 -> x3, other arithmetic: none -> 27.1 us  [derive_regions(): q_next = jnp.sum(lax.all_gather(t0, axis_name=row_axis), axis=0)]
    unnamed x83 -> x77, local copies, waits for them, and re-layouts: 23.7 us -> 21 us
  transfers between devices with their start and end apart: 2 -> 4, of which waited for: 2 -> 4; matrix products, arithmetic and copies ran while one was open for 6% -> 8% of each run, Pallas kernels for 0% -> 0%
where the time goes in v1:
time: 511 us
  waiting for transfers between devices  410 us (80%)
  local copies, waits for them, and re-layouts  34.5 us (7%)
  other arithmetic  32.1 us (6%)
  matrix products  18.2 us (4%)
  between operations  16.2 us (3%)
    all_gather x3, waiting for transfers between devices, derive_regions(): q_next = jnp.sum(lax.all_gather(t0, axis_name=row_axis), axis=0)  367 us
    reduce_scatter x1, waiting for transfers between devices, body(): reduced = lax.psum_scatter(complete, 'win', scatter_dimension=1, tiled=True)  41.6 us
    reduce_sum x3, other arithmetic, derive_regions(): q_next = jnp.sum(lax.all_gather(t0, axis_name=row_axis), axis=0)  27.1 us
    unnamed x77, local copies, waits for them, and re-layouts  21 us
    dot_general x16, matrix products, correlate(): jnp.einsum('pt,gct->pgc', sources[:, offset:offset + time_block], shifted...  18.2 us
  transfers between devices with their start and end apart: 4, of which 4 were waited for; matrix products, arithmetic and copies ran while one was open for 8% of the time, Pallas kernels for 0%

profile of v1, /device:TPU:16, one launch (start us, length us, event | category | flops | bytes accessed | tf_op | source)
XLA Modules:
  0.0 510.6 jit_solution(12498739564118845584)
XLA Ops:
  7.2 1.3 fusion.18
  8.5 1.4 fusion.30
  11.8 2.4 broadcast_select_fusion.2
  19.7 1.4 constant_dynamic-update-slice_fusion.122
  21.9 2.1 constant_dynamic-update-slice_fusion.120
  27.3 1.5 constant_dynamic-update-slice_fusion.104
  28.8 1.7 constant_dynamic-update-slice_fusion.88
  31.0 1.4 constant_dynamic-update-slice_fusion.72
  35.1 1.3 constant_dynamic-update-slice_fusion.48
  38.1 1.2 constant_dynamic-update-slice_fusion.32
  40.2 1.0 constant_dynamic-update-slice_fusion.16
  41.2 110.7 %all-gather.4.cloned.1.call-done = bf16[32,32,8192]{2,1,0:T(8,128)(2,1)} async-done(((bf16[1,32,8192]{2,1,0:T(8,128)(2,1)}), bf16[32,32,8192]{2,1,0:T(8,128)(2,1)}) %all-gather.4.cloned.1.call-update) | async-done | bytes 16777232 | tf_op jit(solution)/shard_map/all_gather | solution.py:11
  151.9 8.9 %reduce_sum.46 = bf16[32,8192]{1,0:T(8,128)(2,1)S(1)} reduce(bf16[32,32,8192]{2,1,0:T(8,128)(2,1)} %all-gather.4.cloned.1.call-done, bf16[]{:T(256)} %constant.21.clone.1), dimensions={0}, to_apply=%region_1.2 | reduce | flops 8126464 | bytes 17301506 | tf_op jit(solution)/shard_map/reduce_sum | solution.py:11
  160.8 127.8 %all-gather.6.cloned.1.call-done = bf16[32,32,8192]{2,1,0:T(8,128)(2,1)} async-done(((bf16[1,32,8192]{2,1,0:T(8,128)(2,1)}), bf16[32,32,8192]{2,1,0:T(8,128)(2,1)}) %all-gather.6.cloned.1.call-update) | async-done | bytes 16777232 | tf_op jit(solution)/shard_map/all_gather | solution.py:11
  288.6 8.7 %reduce_sum.47 = bf16[32,8192]{1,0:T(8,128)(2,1)S(1)} reduce(bf16[32,32,8192]{2,1,0:T(8,128)(2,1)} %all-gather.6.cloned.1.call-done, bf16[]{:T(256)} %constant.21.clone.1), dimensions={0}, to_apply=%region_2.3 | reduce | flops 8126464 | bytes 17301506 | tf_op jit(solution)/shard_map/reduce_sum | solution.py:11
  297.3 128.0 %all-gather.8.cloned.1.call-done = bf16[32,32,8192]{2,1,0:T(8,128)(2,1)} async-done(((bf16[1,32,8192]{2,1,0:T(8,128)(2,1)}), bf16[32,32,8192]{2,1,0:T(8,128)(2,1)}) %all-gather.8.cloned.1.call-update) | async-done | bytes 16777232 | tf_op jit(solution)/shard_map/all_gather | solution.py:11
  425.3 9.5 %reduce_sum.48 = bf16[32,8192]{1,0:T(8,128)(2,1)} reduce(bf16[32,32,8192]{2,1,0:T(8,128)(2,1)} %all-gather.8.cloned.1.call-done, bf16[]{:T(256)} %constant.21.clone.1), dimensions={0}, to_apply=%region_3.4 | reduce | flops 8126464 | bytes 17301506 | tf_op jit(solution)/shard_map/reduce_sum | solution.py:11
  434.8 1.1 pad_maximum_fusion
  440.6 2.3 fusion.26
  442.9 2.3 fusion.27
  445.3 2.3 fusion.28
  447.6 2.5 fusion.29
  460.6 41.6 %reduce-scatter.2.cloned.1.call-done = f32[96,8,32]{0,2,1:T(8,128)} async-done(((f32[96,64,32]{0,2,1:T(8,128)}), f32[96,8,32]{0,2,1:T(8,128)}) %reduce-scatter.2.cloned.1.call-update) | async-done | bytes 98320 | tf_op jit(solution)/shard_map/reduce_scatter | solution.py:64
  502.2 1.8 copy.7
  (98 shorter events, 30.1 us)
Async XLA Ops:
  6.5 145.4 %all-gather.4.cloned.1.call-start = ((), (), s32[]{:S(2)}) async-start(), calls=%async_computation.1 | async-start | bytes 17301504 | tf_op jit(solution)/shard_map/all_gather | solution.py:11
  7.2 8.6 %copy-start = (bf16[1,32,8192]{2,1,0:T(8,128)(2,1)S(1)}, bf16[1,32,8192]{2,1,0:T(8,128)(2,1)}, u32[]{:S(2)}) copy-start(bf16[1,32,8192]{2,1,0:T(8,128)(2,1)} %param.3) | copy-start | bytes 1572868
  14.3 274.3 %all-gather.6.cloned.1.call-start = ((), (), s32[]{:S(2)}) async-start(), calls=%async_computation.2 | async-start | bytes 17301504 | tf_op jit(solution)/shard_map/all_gather | solution.py:11
  15.0 410.3 %all-gather.8.cloned.1.call-start = ((), (), s32[]{:S(2)}) async-start(), calls=%async_computation.3 | async-start | bytes 17301504 | tf_op jit(solution)/shard_map/all_gather | solution.py:11
  15.7 486.5 %reduce-scatter.2.cloned.1.call-start = ((), (), s32[]{:S(2)}) async-start(), calls=%async_computation.4 | async-start | bytes 1179648 | tf_op jit(solution)/shard_map/reduce_scatter | solution.py:64
  21.9 2.5 copy-start.1
  21.9 2.5 copy-start.3
  21.9 3.9 copy-start.5
  21.9 3.9 copy-start.7
  21.9 4.2 copy-start.9
  21.9 4.7 copy-start.11
  24.0 3.3 copy-start.15
  25.5 3.3 copy-start.19
  28.8 2.2 copy-start.17
  30.5 1.8 copy-start.13
  32.4 4.9 copy-start.21
  436.7 1.7 copy-start.4
  438.3 1.6 copy-start.6
  447.6 2.5 copy-start.20
  450.8 1.7 copy-start.10
  453.3 1.8 copy-start.22
  454.8 1.7 copy-start.14
  455.8 1.8 copy-start.18
  457.2 1.7 copy-start.16
  (4 other events, 5.8 us)
Sparse Core Ops, SparseCore 0:
  14.4 137.4 all-gather.3
  154.7 133.8 all-gather.5
  291.4 133.8 all-gather.7
  460.7 41.4 reduce-scatter.1
